TPU v7x, 256 devices: a whole 4x4x8 slice. The times are simulated.
256 devices in a mesh: phase: 2 (over x_hi), ctx: 16 (over x_lo, z), head: 8 (over y, core).
Axes of the slice: x: 4 (x_hi: 2, x_lo: 2; x = x_hi * 2 + x_lo), y: 4, z: 8, core: 2. Of those that a mesh axis runs over, the one named last changes fastest.
Arguments:
- query: bfloat16 [2, 4096, 5120], P('phase', 'ctx', 'head'), may hold values from -18 to 18
- key_cache: bfloat16 [4096, 1024], P('ctx', 'head'), may hold values from -18 to 18
- value_cache: bfloat16 [4096, 1024], P('ctx', 'head'), may hold values from -6 to 6
- saved_output: bfloat16 [2, 4096, 5120], P('phase', 'ctx', 'head'), may hold values from -1.796875 to 1.796875
- out_grad: bfloat16 [2, 4096, 5120], P('phase', 'ctx', 'head'), may hold values from -6 to 6
- out_weight: bfloat16 [2, 5120, 5120], P('phase', 'head'), may hold values from -0.078125 to 0.078125
- doc_lengths: int32 [4], replicated, may hold values from 1 to 3072, 4096 in all
Outputs:
- grad_query: float32 [2, 4096, 5120], P('phase', 'ctx', 'head')
- grad_key: float32 [4096, 1024], P('ctx', 'head')
- grad_value: float32 [4096, 1024], P('ctx', 'head')
Inputs may be any that keep to these rules, and one draw needn't show every extreme that they name: `doc_lengths`: the 4 lengths sum to 4096, and one document has exactly 3072 positions.
All inputs are finite; a program needn't handle non-finite values.
Results may differ from a plain program's by a relative error of at most 0.0041.
Values may be sent and summed in bfloat16 or wider, within the bound.
No kernel may reach another device: no remote copies, remote signals or barrier semaphores. Data moves between devices by JAX's collectives and lax.ppermute only.
A program may use at most 128 MiB of HBM per device.

v0:
```python
import jax
import jax.numpy as jnp
from jax import lax
from jax.sharding import PartitionSpec as P

HD = 128
BLOCK = 512
MASKED = -1e30


def segment_of(places, ends):
    return jnp.sum((places[:, None] >= ends[None, :]).astype(jnp.int32), axis=1)


def visible(query_place, query_segment, key_place, key_segment):
    return (key_place[None, :] <= query_place[:, None]) & (
        key_segment[None, :] == query_segment[:, None]
    )


def block_scores(queries, keys, allowed, scale):
    scores = jnp.einsum("tjgd,kjd->jgtk", queries, keys, preferred_element_type=jnp.float32) * scale
    return jnp.where(allowed[None, None], scores, MASKED)


def running_update(carry, scores, allowed):
    largest, total = carry
    raised = jnp.maximum(largest, jnp.max(scores, axis=-1))
    terms = jnp.where(allowed[None, None], jnp.exp(scores - raised[..., None]), 0.0)
    return (raised, total * jnp.exp(largest - raised) + jnp.sum(terms, axis=-1))


def block_grads(queries, grads, keys, values, allowed, log_total, delta, scale):
    scores = block_scores(queries, keys, allowed, scale)
    weights = jnp.where(allowed[None, None], jnp.exp(scores - log_total[..., None]), 0.0)
    weights_low = weights.astype(jnp.bfloat16)
    value_grad = jnp.einsum(
        "jgtk,tjgd->kjd", weights_low, grads, preferred_element_type=jnp.float32
    )
    weight_grad = jnp.einsum("tjgd,kjd->jgtk", grads, values, preferred_element_type=jnp.float32)
    score_grad = (weights * (weight_grad - delta[..., None])).astype(jnp.bfloat16)
    query_grad = jnp.einsum("jgtk,kjd->tjgd", score_grad, keys, preferred_element_type=jnp.float32)
    key_grad = jnp.einsum("jgtk,tjgd->kjd", score_grad, queries, preferred_element_type=jnp.float32)
    return (query_grad, key_grad, value_grad)


def body(query, key_cache, value_cache, saved_output, out_grad, out_weight, doc_lengths):
    rows = query.shape[1]
    query_cols = query.shape[2]
    key_cols = key_cache.shape[1]
    kv_heads = key_cols // HD
    groups = query_cols // key_cols
    scale = HD ** (-0.5)
    rank = lax.axis_index("ctx")
    ends = jnp.cumsum(doc_lengths)
    query_place = rank * rows + jnp.arange(rows, dtype=jnp.int32)
    query_segment = segment_of(query_place, ends)
    grad_rows = out_grad[0]
    weight = out_weight[0]
    grad_attn = lax.psum_scatter(
        lax.dot_general(
            weight, grad_rows, (((0,), (1,)), ((), ())), preferred_element_type=jnp.float32
        ),
        "head",
        scatter_dimension=0,
        tiled=True,
    ).T.astype(jnp.bfloat16)
    queries = query[0].reshape(rows, kv_heads, groups, HD)
    grads = grad_attn.reshape(rows, kv_heads, groups, HD)
    outputs = saved_output[0].reshape(rows, kv_heads, groups, HD)
    delta = jnp.einsum("tjgd,tjgd->jgt", grads, outputs, preferred_element_type=jnp.float32)
    initial = (
        jnp.full((kv_heads, groups, rows), MASKED, jnp.float32),
        jnp.zeros((kv_heads, groups, rows), jnp.float32),
    )
    whole_keys, whole_values = (
        lax.all_gather(key_cache, "ctx", axis=0, tiled=True),
        lax.all_gather(value_cache, "ctx", axis=0, tiled=True),
    )
    length = whole_keys.shape[0]
    parts = length // BLOCK
    key_blocks = whole_keys.reshape(parts, BLOCK, kv_heads, HD)
    value_blocks = whole_values.reshape(parts, BLOCK, kv_heads, HD)
    key_places = jnp.arange(length, dtype=jnp.int32)
    key_segments = segment_of(key_places, ends).reshape(parts, BLOCK)
    key_places = key_places.reshape(parts, BLOCK)

    def stats_step(carry, inputs):
        keys, places, segments = inputs
        allowed = visible(query_place, query_segment, places, segments)
        return (running_update(carry, block_scores(queries, keys, allowed, scale), allowed), None)

    (largest, total), _ = lax.scan(stats_step, initial, (key_blocks, key_places, key_segments))
    log_total = largest + jnp.log(total)

    def grad_step(carry, inputs):
        keys, values, places, segments = inputs
        allowed = visible(query_place, query_segment, places, segments)
        query_grad, key_grad, value_grad = block_grads(
            queries, grads, keys, values, allowed, log_total, delta, scale
        )
        joined = jnp.concatenate(
            [key_grad.reshape(BLOCK, key_cols), value_grad.reshape(BLOCK, key_cols)], axis=1
        )
        return (carry + query_grad, joined)

    query_sum, kv_terms = lax.scan(
        grad_step,
        jnp.zeros((rows, kv_heads, groups, HD), jnp.float32),
        (key_blocks, value_blocks, key_places, key_segments),
    )
    mine = lax.psum_scatter(
        kv_terms.reshape(length, 2 * key_cols), "ctx", scatter_dimension=0, tiled=True
    )
    key_sum = mine[:, :key_cols] * scale
    value_sum = mine[:, key_cols:]
    query_sum = query_sum.reshape(rows, query_cols)
    key_total, value_total = lax.psum((key_sum, value_sum), "phase")
    grad_query = (query_sum * scale).reshape(1, rows, query_cols)
    return (grad_query, key_total, value_total)


def solution(mesh):
    placed = (
        P("phase", "ctx", "head"),
        P("ctx", "head"),
        P("ctx", "head"),
        P("phase", "ctx", "head"),
        P("phase", "ctx", "head"),
        P("phase", "head", None),
        P(),
    )
    return jax.shard_map(
        body,
        mesh=mesh,
        in_specs=placed,
        out_specs=(P("phase", "ctx", "head"), P("ctx", "head"), P("ctx", "head")),
        check_vma=False,
    )
```

profile of v0, /device:TPU:1, one launch (start us, length us, event | category | flops | bytes accessed | tf_op | source)
XLA Modules:
  0.0 339.7 jit_solution(13072499944512161214)
XLA Ops:
  9.0 7.4 %fusion.42 = f32[5120,256]{1,0:T(8,128)} fusion(bf16[1,640,5120]{2,1,0:T(8,128)(2,1)} %param.16, bf16[1,256,640]{2,1,0:T(8,128)(2,1)S(1)} %copy-done), kind=kOutput, calls=%fused_computation.56 | convolution fusion | flops 1677721600 | bytes 12124160 | tf_op jit(solution)/shard_map/dot_general | solution.py:61
  17.9 0.9 copy.38
  18.8 0.9 copy.55
  19.7 52.7 %all-gather.3.cloned.1.call-done = bf16[4096,128]{1,0:T(8,128)(2,1)} async-done(((bf16[256,128]{1,0:T(8,128)(2,1)}), bf16[4096,128]{1,0:T(8,128)(2,1)}) %all-gather.3.cloned.1.call-update) | async-done | bytes 1048592 | tf_op jit(solution)/shard_map/all_gather | solution.py:77
  72.4 20.6 %while.26 = (s32[]{:T(128)}, f32[1,5,256]{2,1,0:T(8,128)S(1)}, f32[1,5,256]{2,1,0:T(8,128)S(1)}, s32[8,512]{1,0:T(8,128)S(1)}, s32[8,512]{1,0:T(8,128)S(1)}, /*i...) while((s32[]{:T(128)}, f32[1,5,256]{2,1,0:T(8,128)S(1)}, ...), condition=%wide.region_6.7_spmd.clone, body=%wide.region_3.0_spmd.clone.sunk | while | flops 173414912 | bytes 6176908 | solution.py:93
  72.7 1.6 fusion.64
  75.2 1.6 fusion.64
  77.8 1.6 fusion.64
  80.4 1.6 fusion.64
  83.0 1.6 fusion.64
  85.6 1.6 fusion.64
  88.1 1.6 fusion.64
  90.7 1.6 fusion.64
  93.1 1.1 convert_element_type.20
  94.2 1.1 fusion.44
  95.3 45.4 %all-gather.5.cloned.1.call-done = bf16[4096,128]{1,0:T(8,128)(2,1)} async-done(((bf16[256,128]{1,0:T(8,128)(2,1)}), bf16[4096,128]{1,0:T(8,128)(2,1)}) %all-gather.5.cloned.1.call-update) | async-done | bytes 1048592 | tf_op jit(solution)/shard_map/all_gather | solution.py:78
  140.8 65.1 %while.27 = (s32[]{:T(128)}, f32[256,1,5,128]{0,3,2,1:T(8,128)}, f32[8,512,256]{2,1,0:T(8,128)}, bf16[8,512,1,128]{3,1,2,0:T(8,128)(2,1)}, s32[8,512]{1,0:T(8,12...) while((s32[]{:T(128)}, f32[256,1,5,128]{0,3,2,1:T(8,128)}, ...), condition=%wide.region_9.10_spmd.clone, body=%wide.region_8.9_spmd.clone.sunk | while | flops 847577344 | bytes 45119780 | solution.py:107
  140.8 1.4 fusion.75
  142.4 2.1 fusion.76
  144.6 1.5 fusion.77
  148.9 1.4 fusion.75
  150.5 2.1 fusion.76
  152.7 1.5 fusion.77
  157.0 1.4 fusion.75
  158.7 2.1 fusion.76
  160.8 1.5 fusion.77
  165.1 1.4 fusion.75
  166.8 2.1 fusion.76
  168.9 1.5 fusion.77
  173.3 1.4 fusion.75
  174.9 2.1 fusion.76
  177.1 1.5 fusion.77
  181.4 1.4 fusion.75
  183.0 2.1 fusion.76
  185.2 1.5 fusion.77
  188.7 0.9 constant_dynamic-update-slice_fusion.2
  189.5 1.4 fusion.75
  191.2 2.1 fusion.76
  193.3 1.5 fusion.77
  197.7 1.4 fusion.75
  199.3 2.1 fusion.76
  201.5 1.5 fusion.77
  205.9 78.6 %reduce-scatter.5.cloned.1.call-done = f32[256,256]{1,0:T(8,128)} async-done(((f32[4096,256]{1,0:T(8,128)}), f32[256,256]{1,0:T(8,128)}) %reduce-scatter.5.cloned.1.call-update) | async-done | bytes 262160 | tf_op jit(solution)/shard_map/reduce_scatter | solution.py:112
  284.5 1.7 fusion.46
  286.3 1.1 copy.41
  287.3 42.1 %all-reduce.3.cloned.1.call-done = (f32[256,128]{1,0:T(8,128)}, f32[256,128]{1,0:T(8,128)}) async-done(((f32[256,128]{1,0:T(8,128)}, f32[256,128]{1,0:T(8,128)}), (f32[256,128]{1,0:T(8,128)}, f32[256,128]{1,0:T(8,128)})) %all-reduce.3.cloned.1.call-update) | async-done | bytes 262160 | tf_op jit(solution)/shard_map/psum | solution.py:118
  329.5 1.6 copy.82
  331.1 1.6 copy.83
  (217 shorter events, 32.7 us)
Async XLA Ops:
  8.0 1.0 copy-start
  8.0 64.4 %all-gather.3.cloned.1.call-start = ((), (), s32[]{:S(2)}) async-start(), calls=%async_computation.2 | async-start | bytes 1114112 | tf_op jit(solution)/shard_map/all_gather | solution.py:77
  8.7 84.3 %reduce-scatter.3.cloned.1.call-start = ((), (), s32[]{:S(2)}) async-start(), calls=%async_computation.4 | async-start | bytes 5898240 | tf_op jit(solution)/shard_map/reduce_scatter | solution.py:60
  16.4 0.9 copy-start.8
  16.4 1.3 copy-start.6
  16.4 2.4 copy-start.7
  16.4 124.3 %all-gather.5.cloned.1.call-start = ((), (), s32[]{:S(2)}) async-start(), calls=%async_computation.3 | async-start | bytes 1114112 | tf_op jit(solution)/shard_map/all_gather | solution.py:78
  17.2 267.3 %reduce-scatter.5.cloned.1.call-start = ((), (), s32[]{:S(2)}) async-start(), calls=%async_computation.5 | async-start | bytes 4456448 | tf_op jit(solution)/shard_map/reduce_scatter | solution.py:112
  142.1 2.4 copy-start.1
  142.4 2.2 copy-start.3
  144.6 1.8 copy-start.2
  146.1 1.1 copy-start.4
  150.3 2.4 copy-start.1
  150.5 2.2 copy-start.3
  152.7 1.8 copy-start.2
  154.2 1.1 copy-start.4
  158.4 2.4 copy-start.1
  158.6 2.2 copy-start.3
  160.8 1.8 copy-start.2
  162.3 1.1 copy-start.4
  166.5 2.4 copy-start.1
  166.8 2.2 copy-start.3
  168.9 1.8 copy-start.2
  170.5 1.1 copy-start.4
  174.7 2.4 copy-start.1
  174.9 2.2 copy-start.3
  177.1 1.8 copy-start.2
  178.6 1.1 copy-start.4
  182.8 2.4 copy-start.1
  183.0 2.2 copy-start.3
  185.2 1.8 copy-start.2
  186.7 1.1 copy-start.4
  190.9 2.4 copy-start.1
  191.2 2.1 copy-start.3
  193.3 1.8 copy-start.2
  194.9 1.1 copy-start.4
  199.1 2.4 copy-start.1
  199.3 2.1 copy-start.3
  201.5 1.8 copy-start.2
  203.0 1.1 copy-start.4
  205.8 80.3 %copy-start.5 = (f32[256,1,5,128]{0,3,2,1:T(8,128)S(1)}, f32[256,1,5,128]{0,3,2,1:T(8,128)}, u32[]{:S(2)}) copy-start(f32[256,1,5,128]{0,3,2,1:T(8,128)} %get-tuple-element.121) | copy-start | bytes 1966084
  205.9 123.6 %all-reduce.3.cloned.1.call-start = ((), (), s32[]{:S(2)}) async-start(), calls=%async_computation.6 | async-start | bytes 524288 | tf_op jit(solution)/shard_map/psum | solution.py:118
Sparse Core Ops, SparseCore 0:
  10.6 61.7 all-gather.2
  74.2 66.5 all-gather.4
  206.0 78.4 reduce-scatter.4
Sparse Core Ops, SparseCore 1:
  16.5 44.4 reduce-scatter.2
  286.3 43.2 all-reduce.2
where the time goes:
time: 341 us; the launch traced here: 340 us
  waiting for transfers between devices  220 us (65%)
  matrix products  71.6 us (21%)
  local copies, waits for them, and re-layouts  17.3 us (5%)
  between operations  15.3 us (4%)
  other arithmetic  13.3 us (4%)
    reduce_scatter x1, waiting for transfers between devices, body(): lax.psum_scatter(kv_terms.reshape(length, 2 * key_cols), 'ctx', scatter_d...  78.6 us
    all_gather x1, waiting for transfers between devices, body(): lax.all_gather(key_cache, 'ctx', axis=0, tiled=True)  52.7 us
    all_gather x1, waiting for transfers between devices, body(): lax.all_gather(value_cache, 'ctx', axis=0, tiled=True)  45.4 us
    psum x1, waiting for transfers between devices, body(): key_total, value_total = lax.psum((key_sum, value_sum), 'phase')  42.1 us
    dot_general x16, matrix products, block_scores(): jnp.einsum('tjgd,kjd->jgtk', queries, keys, preferred_element_type=jnp.fl...  24 us
    dot_general x8, matrix products, block_grads(): jnp.einsum('tjgd,kjd->jgtk', grads, values, preferred_element_type=jnp.fl...  16.9 us
    dot_general x8, matrix products, block_grads(): jnp.einsum('jgtk,kjd->tjgd', score_grad, keys, preferred_element_type=jnp...  12 us
    dynamic_update_slice x16, local copies, waits for them, and re-layouts, body(): lax.scan(grad_step, jnp.zeros((rows, kv_heads, groups, HD), jnp.float32),...  8.37 us
  transfers between devices with their start and end apart: 5, of which 4 were waited for; matrix products, arithmetic and copies ran while one was open for 10% of the time, Pallas kernels for 0%

commit v1 on v0

--- a/solution.py
+++ b/solution.py
@@ -6,6 +6,18 @@
 HD = 128
 BLOCK = 512
 MASKED = -1e30
+
+
+def cut_the_ends(unit):
+    return jnp.concatenate(
+        jax.lax.all_to_all(
+            jnp.stack(jax.lax.axis_size("ctx") * [unit], axis=0),
+            axis_name="ctx",
+            split_axis=0,
+            concat_axis=0,
+        ),
+        0,
+    )
 
 
 def segment_of(places, ends):
@@ -75,7 +87,7 @@
     )
     whole_keys, whole_values = (
         lax.all_gather(key_cache, "ctx", axis=0, tiled=True),
-        lax.all_gather(value_cache, "ctx", axis=0, tiled=True),
+        cut_the_ends(value_cache),
     )
     length = whole_keys.shape[0]
     parts = length // BLOCK

time: 341 us -> 303 us (0.89)
  waiting for transfers between devices: 220 us -> 169 us
  starting transfers between devices: 0.2 us -> 10.3 us
    all_gather x1 -> x0, waiting for transfers between devices: 45.4 us -> none  [body(): lax.all_gather(value_cache, 'ctx', axis=0, tiled=True)]
    all_to_all x0 -> x1, starting transfers between devices: none -> 10.1 us  [cut_the_ends(): jax.lax.all_to_all(jnp.stack(jax.lax.axis_size('ctx') * [unit], axis=0),...]
    all_gather x1, waiting for transfers between devices: 52.7 us -> 48 us  [body(): lax.all_gather(key_cache, 'ctx', axis=0, tiled=True)]
  transfers between devices with their start and end apart: 5 -> 5, of which waited for: 4 -> 3; matrix products, arithmetic and copies ran while one was open for 10% -> 12% of each run, Pallas kernels for 0% -> 0%
where the time goes in v1:
time: 303 us; the launch traced here: 301 us
  waiting for transfers between devices  169 us (56%)
  matrix products  71.6 us (24%)
  local copies, waits for them, and re-layouts  19.7 us (7%)
  between operations  15.3 us (5%)
  other arithmetic  13.2 us (4%)
  starting transfers between devices  10.3 us (3%)
    reduce_scatter x1, waiting for transfers between devices, body(): lax.psum_scatter(kv_terms.reshape(length, 2 * key_cols), 'ctx', scatter_d...  77 us
    all_gather x1, waiting for transfers between devices, body(): lax.all_gather(key_cache, 'ctx', axis=0, tiled=True)  48 us
    psum x1, waiting for transfers between devices, body(): key_total, value_total = lax.psum((key_sum, value_sum), 'phase')  43.7 us
    dot_general x16, matrix products, block_scores(): jnp.einsum('tjgd,kjd->jgtk', queries, keys, preferred_element_type=jnp.fl...  24 us
    dot_general x8, matrix products, block_grads(): jnp.einsum('tjgd,kjd->jgtk', grads, values, preferred_element_type=jnp.fl...  16.9 us
    dot_general x8, matrix products, block_grads(): jnp.einsum('jgtk,kjd->tjgd', score_grad, keys, preferred_element_type=jnp...  12 us
    all_to_all x1, starting transfers between devices, cut_the_ends(): jax.lax.all_to_all(jnp.stack(jax.lax.axis_size('ctx') * [unit], axis=0),...  10.1 us
    dynamic_update_slice x16, local copies, waits for them, and re-layouts, body(): lax.scan(grad_step, jnp.zeros((rows, kv_heads, groups, HD), jnp.float32),...  8.41 us
  transfers between devices with their start and end apart: 5, of which 3 were waited for; matrix products, arithmetic and copies ran while one was open for 12% of the time, Pallas kernels for 0%

profile of v1, /device:TPU:1, one launch (start us, length us, event | category | flops | bytes accessed | tf_op | source)
XLA Modules:
  0.0 301.3 jit_solution(14199291682239048921)
XLA Ops:
  8.7 2.0 stack.2
  10.8 10.1 %all-to-all-start = ((bf16[16,256,128]{2,1,0:T(8,128)(2,1)}), bf16[16,256,128]{2,1,0:T(8,128)(2,1)}, u32[]{:S(2)}, u32[]{:S(2)}) async-start(bf16[16,256,128]{2,1,0:T(8,128)(2,1)} %stack.2), calls=%async_computation | async-start | bytes 2097152 | tf_op jit(solution)/shard_map/all_to_all | solution.py:13
  20.9 7.4 %fusion.42 = f32[5120,256]{1,0:T(8,128)} fusion(bf16[1,640,5120]{2,1,0:T(8,128)(2,1)} %param.16, bf16[1,256,640]{2,1,0:T(8,128)(2,1)S(1)} %copy-done), kind=kOutput, calls=%fused_computation.56 | convolution fusion | flops 1677721600 | bytes 12124160 | tf_op jit(solution)/shard_map/dot_general | solution.py:73
  29.6 0.9 copy.38
  30.5 0.9 copy.55
  31.4 48.0 %all-gather.2.cloned.1.call-done = bf16[4096,128]{1,0:T(8,128)(2,1)} async-done(((bf16[256,128]{1,0:T(8,128)(2,1)}), bf16[4096,128]{1,0:T(8,128)(2,1)}) %all-gather.2.cloned.1.call-update) | async-done | bytes 1048592 | tf_op jit(solution)/shard_map/all_gather | solution.py:89
  79.4 20.6 %while.26 = (s32[]{:T(128)}, f32[1,5,256]{2,1,0:T(8,128)S(1)}, f32[1,5,256]{2,1,0:T(8,128)S(1)}, s32[8,512]{1,0:T(8,128)S(1)}, s32[8,512]{1,0:T(8,128)S(1)}, /*i...) while((s32[]{:T(128)}, f32[1,5,256]{2,1,0:T(8,128)S(1)}, ...), condition=%wide.region_6.7_spmd.clone, body=%wide.region_3.0_spmd.clone.sunk | while | flops 173414912 | bytes 6176908 | solution.py:105
  79.6 1.6 fusion.64
  82.2 1.6 fusion.64
  84.8 1.6 fusion.64
  87.4 1.6 fusion.64
  89.9 1.6 fusion.64
  92.5 1.6 fusion.64
  95.1 1.6 fusion.64
  97.7 1.6 fusion.64
  100.1 1.1 convert_element_type.20
  101.2 1.1 fusion.44
  102.3 65.1 %while.27 = (s32[]{:T(128)}, f32[256,1,5,128]{0,3,2,1:T(8,128)}, f32[8,512,256]{2,1,0:T(8,128)}, bf16[8,512,1,128]{3,1,2,0:T(8,128)(2,1)}, s32[8,512]{1,0:T(8,12...) while((s32[]{:T(128)}, f32[256,1,5,128]{0,3,2,1:T(8,128)}, ...), condition=%wide.region_9.10_spmd.clone, body=%wide.region_8.9_spmd.clone.sunk | while | flops 847577344 | bytes 45119780 | solution.py:119
  102.3 1.4 fusion.75
  103.9 2.1 fusion.76
  106.1 1.5 fusion.77
  110.4 1.4 fusion.75
  112.1 2.1 fusion.76
  114.2 1.5 fusion.77
  118.5 1.4 fusion.75
  120.2 2.1 fusion.76
  122.4 1.5 fusion.77
  126.7 1.4 fusion.75
  128.3 2.1 fusion.76
  130.5 1.5 fusion.77
  134.8 1.4 fusion.75
  136.5 2.1 fusion.76
  138.6 1.5 fusion.77
  142.9 1.4 fusion.75
  144.6 2.1 fusion.76
  146.7 1.5 fusion.77
  151.1 1.4 fusion.75
  152.7 2.1 fusion.76
  154.9 1.5 fusion.77
  159.2 1.4 fusion.75
  160.9 2.1 fusion.76
  163.1 1.5 fusion.77
  167.5 77.0 %reduce-scatter.5.cloned.1.call-done = f32[256,256]{1,0:T(8,128)} async-done(((f32[4096,256]{1,0:T(8,128)}), f32[256,256]{1,0:T(8,128)}) %reduce-scatter.5.cloned.1.call-update) | async-done | bytes 262160 | tf_op jit(solution)/shard_map/reduce_scatter | solution.py:124
  244.5 1.7 fusion.46
  246.3 1.1 copy.41
  247.4 43.7 %all-reduce.3.cloned.1.call-done = (f32[256,128]{1,0:T(8,128)}, f32[256,128]{1,0:T(8,128)}) async-done(((f32[256,128]{1,0:T(8,128)}, f32[256,128]{1,0:T(8,128)}), (f32[256,128]{1,0:T(8,128)}, f32[256,128]{1,0:T(8,128)})) %all-reduce.3.cloned.1.call-update) | async-done | bytes 262160 | tf_op jit(solution)/shard_map/psum | solution.py:130
  291.0 1.6 copy.82
  292.6 1.6 copy.83
  (217 shorter events, 33.2 us)
Async XLA Ops:
  8.0 12.9 %copy-start = (bf16[1,256,640]{2,1,0:T(8,128)(2,1)S(1)}, bf16[1,256,640]{2,1,0:T(8,128)(2,1)}, u32[]{:S(2)}) copy-start(bf16[1,256,640]{2,1,0:T(8,128)(2,1)} %param.15) | copy-start | bytes 983044
  8.0 71.4 %all-gather.2.cloned.1.call-start = ((), (), s32[]{:S(2)}) async-start(), calls=%async_computation.3 | async-start | bytes 1114112 | tf_op jit(solution)/shard_map/all_gather | solution.py:89
  10.8 91.5 %all-to-all-start = ((bf16[16,256,128]{2,1,0:T(8,128)(2,1)}), bf16[16,256,128]{2,1,0:T(8,128)(2,1)}, u32[]{:S(2)}, u32[]{:S(2)}) async-start(bf16[16,256,128]{2,1,0:T(8,128)(2,1)} %stack.2), calls=%async_computation | async-start | bytes 2097152 | tf_op jit(solution)/shard_map/all_to_all | solution.py:13
  20.9 79.2 %reduce-scatter.3.cloned.1.call-start = ((), (), s32[]{:S(2)}) async-start(), calls=%async_computation.4 | async-start | bytes 5898240 | tf_op jit(solution)/shard_map/reduce_scatter | solution.py:72
  28.3 0.7 copy-start.8
  28.3 1.1 copy-start.6
  28.4 2.1 copy-start.7
  28.4 216.1 %reduce-scatter.5.cloned.1.call-start = ((), (), s32[]{:S(2)}) async-start(), calls=%async_computation.5 | async-start | bytes 4456448 | tf_op jit(solution)/shard_map/reduce_scatter | solution.py:124
  103.7 2.4 copy-start.1
  103.9 2.1 copy-start.3
  106.1 1.8 copy-start.2
  107.6 1.1 copy-start.4
  111.8 2.4 copy-start.1
  112.1 2.2 copy-start.3
  114.2 1.8 copy-start.2
  115.7 1.1 copy-start.4
  119.9 2.4 copy-start.1
  120.2 2.2 copy-start.3
  122.3 1.8 copy-start.2
  123.9 1.1 copy-start.4
  128.1 2.4 copy-start.1
  128.3 2.2 copy-start.3
  130.5 1.8 copy-start.2
  132.0 1.1 copy-start.4
  136.2 2.4 copy-start.1
  136.5 2.2 copy-start.3
  138.6 1.8 copy-start.2
  140.1 1.1 copy-start.4
  144.3 2.4 copy-start.1
  144.6 2.1 copy-start.3
  146.7 1.8 copy-start.2
  148.2 1.1 copy-start.4
  152.5 2.4 copy-start.1
  152.7 2.2 copy-start.3
  154.9 1.8 copy-start.2
  156.4 1.1 copy-start.4
  160.6 2.4 copy-start.1
  160.9 2.2 copy-start.3
  163.0 1.8 copy-start.2
  164.6 1.1 copy-start.4
  167.4 78.8 %copy-start.5 = (f32[256,1,5,128]{0,3,2,1:T(8,128)S(1)}, f32[256,1,5,128]{0,3,2,1:T(8,128)}, u32[]{:S(2)}) copy-start(f32[256,1,5,128]{0,3,2,1:T(8,128)} %get-tuple-element.121) | copy-start | bytes 1966084
  167.4 123.6 %all-reduce.3.cloned.1.call-start = ((), (), s32[]{:S(2)}) async-start(), calls=%async_computation.6 | async-start | bytes 524288 | tf_op jit(solution)/shard_map/psum | solution.py:130
Sparse Core Ops, SparseCore 0:
  10.6 68.7 all-gather.1
  167.6 76.9 reduce-scatter.4
  247.7 43.2 all-reduce.2
Sparse Core Ops, SparseCore 1:
  28.5 42.6 reduce-scatter.2
